TPU v7x, 256 devices: a whole 4x4x8 slice. The times are simulated.
256 devices in a mesh: scan: 8 (over x, core), mode: 32 (over y, z).
Axes of the slice: x: 4, y: 4, z: 8, core: 2. Of those that a mesh axis runs over, the one named last changes fastest.
Arguments:
- object_field: float32 [2, 2048, 1024], P(None, 'scan'), may hold values from -5 to 5
- probe_modes: float32 [2, 32, 128, 128], P(None, 'mode'), may hold values from -9 to 9
- scan_offsets: int32 [2, 256], P(None, 'scan'), may hold values from 0 to 896, as said below
- measured: float32 [256, 128, 128], P('scan'), may hold values from 0.05 to 3
Outputs:
- object_new: float32 [2, 2048, 1024], P(None, ('scan', 'mode'))
- probe_new: float32 [2, 32, 128, 128], P(None, 'mode')
Inputs may be any that keep to these rules, and one draw needn't show every extreme that they name: scan_offsets[0, j] lies in 0 to 128 and scan_offsets[1, j] in 0 to 896; position j belongs to tile j // 32.
All inputs are finite; a program needn't handle non-finite values.
Results may differ from a plain program's by a relative error of at most 0.0027.
Values sent between devices are 32-bit elements; how exact they have to be, the bound alone decides.
No kernel may reach another device: no remote copies, remote signals or barrier semaphores. Data moves between devices by JAX's collectives and lax.ppermute only.
A program may use at most 128 MiB of HBM per device.

v0:
```python
import math

import jax
import jax.numpy as jnp
from jax import lax
from jax.sharding import PartitionSpec as P

M = 128
NS_ITERS = 8


FLOOR_INTENSITY = 0.1
FLOOR_ILLUM = 1.0
EPSILON = 1e-06


def dft_tables(length):
    pixel_index = jnp.arange(length, dtype=jnp.int32)
    product = pixel_index[:, None] * pixel_index[None, :] % length
    phase_angle = product.astype(jnp.float32) * (2.0 * math.pi / length)
    norm_scale = 1.0 / math.sqrt(length)
    return (
        (jnp.cos(phase_angle) * norm_scale).astype(jnp.bfloat16),
        (-jnp.sin(phase_angle) * norm_scale).astype(jnp.bfloat16),
    )


def right_product(left, table):
    return jnp.einsum("nab,bc->nac", left, table, preferred_element_type=jnp.float32)


def left_product(table, right):
    return jnp.einsum("ab,nbc->nac", table, right, preferred_element_type=jnp.float32)


def forward_pass(wave_re, wave_im, cos_t, sin_t):
    mid_re = (right_product(wave_re, cos_t) - right_product(wave_im, sin_t)).astype(jnp.bfloat16)
    mid_im = (right_product(wave_re, sin_t) + right_product(wave_im, cos_t)).astype(jnp.bfloat16)
    far_re = left_product(cos_t, mid_re) - left_product(sin_t, mid_im)
    far_im = left_product(sin_t, mid_re) + left_product(cos_t, mid_im)
    return (far_re, far_im)


def inverse_pass(spec_re, spec_im, cos_t, sin_t):
    half_re = (right_product(spec_re, cos_t) + right_product(spec_im, sin_t)).astype(jnp.bfloat16)
    half_im = (right_product(spec_im, cos_t) - right_product(spec_re, sin_t)).astype(jnp.bfloat16)
    back_re = left_product(cos_t, half_re) + left_product(sin_t, half_im)
    back_im = left_product(cos_t, half_im) - left_product(sin_t, half_re)
    return (back_re, back_im)


def highest_dot(left, right):
    return jnp.dot(left, right, precision=lax.Precision.HIGHEST, preferred_element_type=jnp.float32)


def gram_of(flat_re, flat_im):
    gram_re = highest_dot(flat_re, flat_re.T) + highest_dot(flat_im, flat_im.T)
    gram_im = highest_dot(flat_re, flat_im.T) - highest_dot(flat_im, flat_re.T)
    return (gram_re, gram_im)


def orthogonal_mix(gram_re, gram_im):
    mode_count = gram_re.shape[0]
    mode_power = jnp.diagonal(gram_re) + EPSILON
    inv_root = 1.0 / jnp.sqrt(mode_power)
    scale_mat = inv_root[:, None] * inv_root[None, :]
    norm_re = gram_re * scale_mat
    norm_im = gram_im * scale_mat
    embedded = jnp.concatenate(
        [jnp.concatenate([norm_re, -norm_im], axis=1), jnp.concatenate([norm_im, norm_re], axis=1)],
        axis=0,
    )
    frobenius = jnp.sqrt(jnp.sum(embedded * embedded))
    identity_mat = jnp.eye(2 * mode_count, dtype=jnp.float32)
    iterate_y = embedded / frobenius
    iterate_z = identity_mat
    for sweep_index in range(NS_ITERS):
        correction = 1.5 * identity_mat - 0.5 * highest_dot(iterate_z, iterate_y)
        iterate_y = highest_dot(iterate_y, correction)
        iterate_z = highest_dot(correction, iterate_z)
    root_inv = iterate_z / jnp.sqrt(frobenius)
    weight_re = root_inv[:mode_count, :mode_count]
    weight_im = root_inv[mode_count:, :mode_count]
    ratio_mat = inv_root[:, None] * jnp.sqrt(mode_power)[None, :]
    return (weight_re * ratio_mat, weight_im * ratio_mat)


def shards(object_field, probe_modes, scan_offsets, measured):
    mode_index = lax.axis_index("mode")
    cos_t, sin_t = dft_tables(M)
    probe_re = probe_modes[0, 0]
    probe_im = probe_modes[1, 0]
    row_starts = scan_offsets[0]
    col_starts = scan_offsets[1]
    local_count = row_starts.shape[0]
    zero_index = jnp.zeros((), jnp.int32)

    def cut_patch(row_start, col_start):
        return lax.dynamic_slice(object_field, (zero_index, row_start, col_start), (2, M, M))

    obj_patches = jax.vmap(cut_patch)(row_starts, col_starts)
    obj_re = obj_patches[:, 0]
    obj_im = obj_patches[:, 1]
    obj_norm = jnp.sum(obj_re * obj_re + obj_im * obj_im, axis=0)
    wave_re = (probe_re * obj_re - probe_im * obj_im).astype(jnp.bfloat16)
    wave_im = (probe_re * obj_im + probe_im * obj_re).astype(jnp.bfloat16)
    far_re, far_im = forward_pass(wave_re, wave_im, cos_t, sin_t)
    mode_intensity = far_re * far_re + far_im * far_im
    intensity = lax.psum(mode_intensity, "mode")
    amp_ratio = jnp.sqrt(measured / jnp.maximum(intensity, FLOOR_INTENSITY))
    factor = amp_ratio - 1.0
    spec_re = (factor * far_re).astype(jnp.bfloat16)
    spec_im = (factor * far_im).astype(jnp.bfloat16)
    back_re, back_im = inverse_pass(spec_re, spec_im, cos_t, sin_t)
    grad_re = jnp.sum(obj_re * back_re + obj_im * back_im, axis=0)
    grad_im = jnp.sum(obj_re * back_im - obj_im * back_re, axis=0)
    patch_re = probe_re * back_re + probe_im * back_im
    patch_im = probe_re * back_im - probe_im * back_re
    light_patch = (probe_re * probe_re + probe_im * probe_im)[None]
    grad_re, grad_im, obj_norm = lax.psum((grad_re, grad_im, obj_norm), "scan")
    step_re = probe_re + grad_re / (obj_norm + EPSILON)
    step_im = probe_im + grad_im / (obj_norm + EPSILON)

    def add_patch(position, state_pair):
        grad_tile, light_tile = state_pair
        row_start = row_starts[position]
        col_start = col_starts[position]
        old_grad = lax.dynamic_slice(grad_tile, (zero_index, row_start, col_start), (2, M, M))
        new_grad = old_grad + jnp.stack([patch_re[position], patch_im[position]])
        grad_tile = lax.dynamic_update_slice(
            grad_tile, new_grad, (zero_index, row_start, col_start)
        )
        old_light = lax.dynamic_slice(light_tile, (zero_index, row_start, col_start), (1, M, M))
        light_tile = lax.dynamic_update_slice(
            light_tile, old_light + light_patch, (zero_index, row_start, col_start)
        )
        return (grad_tile, light_tile)

    tile_shape = object_field.shape
    empty_grad = jnp.zeros(tile_shape, jnp.float32)
    empty_light = jnp.zeros((1, tile_shape[1], tile_shape[2]), jnp.float32)
    grad_tile, light_tile = lax.fori_loop(0, local_count, add_patch, (empty_grad, empty_light))
    grad_rows, light_rows = (
        lax.psum_scatter(grad_tile, "mode", scatter_dimension=1, tiled=True),
        lax.psum_scatter(light_tile, "mode", scatter_dimension=1, tiled=True),
    )
    rows_share = grad_rows.shape[1]
    own_rows = lax.dynamic_slice_in_dim(object_field, mode_index * rows_share, rows_share, 1)
    object_new = own_rows + grad_rows / jnp.maximum(light_rows, FLOOR_ILLUM)
    flat_mine = jnp.stack([step_re.reshape(-1), step_im.reshape(-1)])[:, None, :]
    every_mode = lax.all_gather(flat_mine, "mode", axis=1, tiled=True)
    gathered_re = every_mode[0]
    gathered_im = every_mode[1]
    gram_re, gram_im = gram_of(gathered_re, gathered_im)
    mix_re, mix_im = orthogonal_mix(gram_re, gram_im)
    column_re = lax.dynamic_slice_in_dim(mix_re, mode_index, 1, 1)
    column_im = lax.dynamic_slice_in_dim(mix_im, mode_index, 1, 1)
    mine_re = highest_dot(column_re.T, gathered_re) - highest_dot(column_im.T, gathered_im)
    mine_im = highest_dot(column_re.T, gathered_im) + highest_dot(column_im.T, gathered_re)
    mine = jnp.stack([mine_re, mine_im])
    probe_new = mine.reshape(2, 1, M, M)
    return (object_new, probe_new)


def solution(mesh):
    placed = (
        P(None, "scan", None),
        P(None, "mode", None, None),
        P(None, "scan"),
        P("scan", None, None),
    )
    return jax.shard_map(
        shards,
        mesh=mesh,
        in_specs=placed,
        out_specs=(P(None, ("scan", "mode"), None), P(None, "mode", None, None)),
        check_vma=False,
    )
```

profile of v0, /device:TPU:2, one launch (start us, length us, event | category | flops | bytes accessed | tf_op | source)
XLA Modules:
  0.0 1224.2 jit_solution(16505864127190747338)
XLA Ops:
  9.1 119.1 %while.17 = (s32[]{:T(128)}, f32[2,256,1024]{2,1,0:T(8,128)}, s32[32,3]{0,1:T(4,128)S(1)}, f32[32,2,128,128]{2,3,0,1:T(8,128)}, s32[]{:T(128)}) while((s32[]{:T(128)}, f32[2,256,1024]{2,1,0:T(8,128)}, s32[32,3]{0,1:T(4,128)S(1)}, f32[32,2,128,128]{2,3,0,1:T(8,128)}, s32[]{:T(128)}) %tuple.72), condition=%wide.while_cond, body=%wide.while_body.sunk | while | flops 2 | bytes 787057 | solution.py:99
  9.7 2.3 dynamic-slice_bitcast_fusion.2
  13.4 2.3 dynamic-slice_bitcast_fusion.2
  17.2 2.3 dynamic-slice_bitcast_fusion.2
  20.9 2.3 dynamic-slice_bitcast_fusion.2
  24.6 2.3 dynamic-slice_bitcast_fusion.2
  28.3 2.3 dynamic-slice_bitcast_fusion.2
  32.0 2.3 dynamic-slice_bitcast_fusion.2
  35.8 2.3 dynamic-slice_bitcast_fusion.2
  39.5 2.3 dynamic-slice_bitcast_fusion.2
  43.2 2.3 dynamic-slice_bitcast_fusion.2
  46.9 2.3 dynamic-slice_bitcast_fusion.2
  50.7 2.3 dynamic-slice_bitcast_fusion.2
  54.4 2.3 dynamic-slice_bitcast_fusion.2
  58.1 2.3 dynamic-slice_bitcast_fusion.2
  61.9 2.3 dynamic-slice_bitcast_fusion.2
  65.6 2.3 dynamic-slice_bitcast_fusion.2
  69.3 2.3 dynamic-slice_bitcast_fusion.2
  73.0 2.3 dynamic-slice_bitcast_fusion.2
  76.7 2.3 dynamic-slice_bitcast_fusion.2
  80.5 2.3 dynamic-slice_bitcast_fusion.2
  84.2 2.3 dynamic-slice_bitcast_fusion.2
  87.9 2.3 dynamic-slice_bitcast_fusion.2
  91.6 2.3 dynamic-slice_bitcast_fusion.2
  95.3 2.3 dynamic-slice_bitcast_fusion.2
  99.0 2.3 dynamic-slice_bitcast_fusion.2
  102.8 2.3 dynamic-slice_bitcast_fusion.2
  106.5 2.3 dynamic-slice_bitcast_fusion.2
  110.2 2.3 dynamic-slice_bitcast_fusion.2
  113.9 2.3 dynamic-slice_bitcast_fusion.2
  117.7 2.3 dynamic-slice_bitcast_fusion.2
  121.4 2.3 dynamic-slice_bitcast_fusion.2
  125.1 2.3 dynamic-slice_bitcast_fusion.2
  128.2 2.8 fusion.12
  135.9 2.8 fusion.6
  139.0 2.9 copy.91
  142.0 154.1 %all-reduce.4.cloned.1.call-done = f32[32,128,128]{1,2,0:T(8,128)} async-done(((f32[32,128,128]{1,2,0:T(8,128)}), f32[32,128,128]{1,2,0:T(8,128)}) %all-reduce.4.cloned.1.call-update) | async-done | bytes 2097168 | tf_op jit(solution)/shard_map/psum | solution.py:109
  296.1 4.0 fusion.8
  306.4 4.7 fusion.3
  311.6 333.2 %while.16 = (s32[]{:T(128)}, f32[2,256,1024]{2,1,0:T(8,128)S(1)}, f32[1,256,1024]{2,1,0:T(8,128)S(1)}, s32[32]{0:T(128)S(1)}, s32[32]{0:T(128)S(1)}, /*index=5*/...) while((s32[]{:T(128)}, f32[2,256,1024]{2,1,0:T(8,128)S(1)}, ...), condition=%wide.region_2.3_spmd, body=%wide.region_1.2_spmd.sunk | while | flops 81928 | bytes 1507565 | solution.py:142
  357.5 2.3 dynamic_update_slice.16
  378.1 2.3 dynamic_update_slice.16
  388.6 2.5 dynamic_update_slice.16
  409.6 2.5 dynamic_update_slice.16
  420.4 2.4 dynamic_update_slice.16
  431.2 2.4 dynamic_update_slice.16
  441.9 2.4 dynamic_update_slice.16
  462.8 2.4 dynamic_update_slice.16
  493.8 2.4 dynamic_update_slice.16
  504.5 2.4 dynamic_update_slice.16
  515.2 2.4 dynamic_update_slice.16
  566.6 2.4 dynamic_update_slice.16
  577.3 2.4 dynamic_update_slice.16
  587.8 2.5 dynamic_update_slice.16
  608.8 2.3 dynamic_update_slice.16
  619.3 2.5 dynamic_update_slice.16
  640.2 2.5 dynamic_update_slice.16
  648.7 212.6 %reduce-scatter.5.cloned.1.call-done = f32[1,8,1024]{2,1,0:T(8,128)} async-done(((f32[1,256,1024]{2,1,0:T(8,128)}), f32[1,8,1024]{2,1,0:T(8,128)}) %reduce-scatter.5.cloned.1.call-update) | async-done | bytes 32784 | tf_op jit(solution)/shard_map/reduce_scatter | solution.py:145
  862.1 219.8 %reduce-scatter.3.cloned.1.call-done = f32[2,8,1024]{2,1,0:T(8,128)} async-done(((f32[2,256,1024]{2,1,0:T(8,128)}), f32[2,8,1024]{2,1,0:T(8,128)}) %reduce-scatter.3.cloned.1.call-update) | async-done | bytes 65552 | tf_op jit(solution)/shard_map/reduce_scatter | solution.py:144
  1083.4 81.6 %all-gather.3.cloned.1.call-done = f32[2,524288]{1,0:T(2,128)} async-done(((f32[2,16384]{1,0:T(2,128)}), f32[2,524288]{1,0:T(2,128)}) %all-gather.3.cloned.1.call-update) | async-done | bytes 4194320 | tf_op jit(solution)/shard_map/all_gather | solution.py:151
  1165.0 26.1 %slice_reduce_fusion.1 = (f32[524288]{0:T(1024)}, f32[524288]{0:T(1024)}) fusion(f32[2,524288]{1,0:T(2,128)} %all-gather.3.cloned.1.call-done), kind=kLoop, calls=%fused_computation.9 | loop fusion | bytes 8388608 | tf_op jit(solution)/shard_map/slice | solution.py:152
  1192.9 2.8 squeeze.45
  1201.8 3.4 fusion.151
  1211.0 2.7 fusion.78
  (497 shorter events, 250.9 us)
Async XLA Ops:
  7.2 289.0 %all-reduce.4.cloned.1.call-start = ((), (), s32[]{:S(2)}) async-start(), calls=%async_computation.2 | async-start | bytes 4194304 | tf_op jit(solution)/shard_map/psum | solution.py:109
  8.3 296.7 %copy-start.5 = (f32[1,1,128,128]{2,3,1,0:T(8,128)}, f32[1,1,128,128]{2,3,1,0:T(8,128)S(1)}, u32[]{:S(2)}) copy-start(f32[1,1,128,128]{2,3,1,0:T(8,128)S(1)} %copy.128) | copy-start | bytes 196612
  138.7 508.0 %all-reduce.6.cloned.1.call-start = ((), (), s32[]{:S(2)}) async-start(), calls=%async_computation.6 | async-start | bytes 393216 | tf_op jit(solution)/shard_map/psum | solution.py:120
  138.9 3.0 copy-start.7
  304.3 2.2 copy-start.3
  311.2 550.2 %reduce-scatter.5.cloned.1.call-start = ((), (), s32[]{:S(2)}) async-start(), calls=%async_computation.4 | async-start | bytes 1081344 | tf_op jit(solution)/shard_map/reduce_scatter | solution.py:145
  644.8 1.0 copy-start.4
  644.8 1.6 copy-start.2
  644.8 1.9 copy-start.6
  645.8 436.0 %reduce-scatter.3.cloned.1.call-start = ((), (), s32[]{:S(2)}) async-start(), calls=%async_computation.3 | async-start | bytes 2162688 | tf_op jit(solution)/shard_map/reduce_scatter | solution.py:144
  646.5 518.5 %all-gather.3.cloned.1.call-start = ((), (), s32[]{:S(2)}) async-start(), calls=%async_computation.5 | async-start | bytes 4325376 | tf_op jit(solution)/shard_map/all_gather | solution.py:151
  1195.7 1.8 copy-start
  1213.7 2.2 copy-start.1
Sparse Core Ops, SparseCore 0:
  138.8 157.2 all-reduce.3
  311.3 60.6 all-reduce.5
  645.9 215.3 reduce-scatter.4
  865.0 216.7 reduce-scatter.2
  1084.9 80.0 all-gather.2
where the time goes:
time: 1230 us; the launch traced here: 1220 us
  waiting for transfers between devices  668 us (54%)
  local copies, waits for them, and re-layouts  363 us (30%)
  loops' own time  122 us (10%)
  matrix products  35.8 us (3%)
  other arithmetic  20 us (2%)
  between operations  15.1 us (1%)
    reduce_scatter x1, waiting for transfers between devices, shards(): lax.psum_scatter(grad_tile, 'mode', scatter_dimension=1, tiled=True)  220 us
    reduce_scatter x1, waiting for transfers between devices, shards(): lax.psum_scatter(light_tile, 'mode', scatter_dimension=1, tiled=True)  213 us
    psum x1, waiting for transfers between devices, shards(): intensity = lax.psum(mode_intensity, 'mode')  154 us
    another operation x1, loops' own time, shards(): lax.fori_loop(0, local_count, add_patch, (empty_grad, empty_light))  121 us
    gather x160, local copies, waits for them, and re-layouts  119 us
    all_gather x1, waiting for transfers between devices, shards(): every_mode = lax.all_gather(flat_mine, 'mode', axis=1, tiled=True)  81.6 us
    dynamic_update_slice x32, local copies, waits for them, and re-layouts, add_patch(): lax.dynamic_update_slice(grad_tile, new_grad, (zero_index, row_start, col...  73.2 us
    dynamic_update_slice x32, local copies, waits for them, and re-layouts, add_patch(): lax.dynamic_update_slice(light_tile, old_light + light_patch, (zero_index...  59.2 us
  transfers between devices with their start and end apart: 5, of which 4 were waited for; matrix products, arithmetic and copies ran while one was open for 18% of the time, Pallas kernels for 0%

commit v1 on v0

--- a/solution.py
+++ b/solution.py
@@ -85,6 +85,20 @@
     return (weight_re * ratio_mat, weight_im * ratio_mat)
 
 
+def onehot_place(starts, out_len, in_len):
+    out_index = jnp.arange(out_len, dtype=jnp.int32)[None, :, None]
+    in_index = jnp.arange(in_len, dtype=jnp.int32)[None, None, :]
+    return (out_index == starts[:, None, None] + in_index).astype(jnp.bfloat16)
+
+
+def split_parts(values):
+    high = values.astype(jnp.bfloat16)
+    rest = values - high.astype(jnp.float32)
+    middle = rest.astype(jnp.bfloat16)
+    low = (rest - middle.astype(jnp.float32)).astype(jnp.bfloat16)
+    return jnp.stack([high, middle, low])
+
+
 def shards(object_field, probe_modes, scan_offsets, measured):
     mode_index = lax.axis_index("mode")
     cos_t, sin_t = dft_tables(M)
@@ -106,7 +120,10 @@
     wave_im = (probe_re * obj_im + probe_im * obj_re).astype(jnp.bfloat16)
     far_re, far_im = forward_pass(wave_re, wave_im, cos_t, sin_t)
     mode_intensity = far_re * far_re + far_im * far_im
-    intensity = lax.psum(mode_intensity, "mode")
+    own_light = (probe_re * probe_re + probe_im * probe_im)[None]
+    summed = lax.psum(jnp.concatenate([mode_intensity, own_light]), "mode")
+    intensity = summed[:local_count]
+    light_patch = summed[local_count:]
     amp_ratio = jnp.sqrt(measured / jnp.maximum(intensity, FLOOR_INTENSITY))
     factor = amp_ratio - 1.0
     spec_re = (factor * far_re).astype(jnp.bfloat16)
@@ -116,35 +133,29 @@
     grad_im = jnp.sum(obj_re * back_im - obj_im * back_re, axis=0)
     patch_re = probe_re * back_re + probe_im * back_im
     patch_im = probe_re * back_im - probe_im * back_re
-    light_patch = (probe_re * probe_re + probe_im * probe_im)[None]
     grad_re, grad_im, obj_norm = lax.psum((grad_re, grad_im, obj_norm), "scan")
     step_re = probe_re + grad_re / (obj_norm + EPSILON)
     step_im = probe_im + grad_im / (obj_norm + EPSILON)
 
-    def add_patch(position, state_pair):
-        grad_tile, light_tile = state_pair
-        row_start = row_starts[position]
-        col_start = col_starts[position]
-        old_grad = lax.dynamic_slice(grad_tile, (zero_index, row_start, col_start), (2, M, M))
-        new_grad = old_grad + jnp.stack([patch_re[position], patch_im[position]])
-        grad_tile = lax.dynamic_update_slice(
-            grad_tile, new_grad, (zero_index, row_start, col_start)
-        )
-        old_light = lax.dynamic_slice(light_tile, (zero_index, row_start, col_start), (1, M, M))
-        light_tile = lax.dynamic_update_slice(
-            light_tile, old_light + light_patch, (zero_index, row_start, col_start)
-        )
-        return (grad_tile, light_tile)
-
-    tile_shape = object_field.shape
-    empty_grad = jnp.zeros(tile_shape, jnp.float32)
-    empty_light = jnp.zeros((1, tile_shape[1], tile_shape[2]), jnp.float32)
-    grad_tile, light_tile = lax.fori_loop(0, local_count, add_patch, (empty_grad, empty_light))
-    grad_rows, light_rows = (
-        lax.psum_scatter(grad_tile, "mode", scatter_dimension=1, tiled=True),
-        lax.psum_scatter(light_tile, "mode", scatter_dimension=1, tiled=True),
-    )
-    rows_share = grad_rows.shape[1]
+    rows_share = object_field.shape[1] // lax.axis_size("mode")
+    col_place = onehot_place(col_starts, object_field.shape[2], M)
+    row_place = onehot_place(row_starts, object_field.shape[1], M)
+    patch_parts = split_parts(jnp.stack([patch_re, patch_im]))
+    placed_rows = jnp.einsum(
+        "jia,pcjab->pcjib", row_place, patch_parts, preferred_element_type=jnp.float32
+    ).astype(jnp.bfloat16)
+    grad_tile = jnp.einsum(
+        "pcjib,jkb->pcik", placed_rows, col_place, preferred_element_type=jnp.float32
+    ).sum(axis=0)
+    own_place = onehot_place(row_starts - mode_index * rows_share, rows_share, M)
+    light_parts = split_parts(light_patch[0])
+    light_rows = jnp.einsum(
+        "jia,pab->pjib", own_place, light_parts, preferred_element_type=jnp.float32
+    ).astype(jnp.bfloat16)
+    light_rows = jnp.einsum(
+        "pjib,jkb->pik", light_rows, col_place, preferred_element_type=jnp.float32
+    ).sum(axis=0)[None]
+    grad_rows = lax.psum_scatter(grad_tile, "mode", scatter_dimension=1, tiled=True)
     own_rows = lax.dynamic_slice_in_dim(object_field, mode_index * rows_share, rows_share, 1)
     object_new = own_rows + grad_rows / jnp.maximum(light_rows, FLOOR_ILLUM)
     flat_mine = jnp.stack([step_re.reshape(-1), step_im.reshape(-1)])[:, None, :]

time: 1230 us -> 751 us (0.61)
  local copies, waits for them, and re-layouts: 363 us -> 155 us
  waiting for transfers between devices: 668 us -> 493 us
  loops' own time: 122 us -> 0.4 us
  matrix products: 35.8 us -> 56.5 us
    reduce_scatter x1 -> x0, waiting for transfers between devices: 213 us -> none  [shards(): lax.psum_scatter(light_tile, 'mode', scatter_dimension=1, tiled=True)]
    dynamic_update_slice x64 -> x0, local copies, waits for them, and re-layouts: 132 us -> none  [the longest x32 73.2 us: add_patch(): lax.dynamic_update_slice(grad_tile, new_grad, (zero_index, row_start, col...]
    another operation x1 -> x0, loops' own time: 121 us -> none  [shards(): lax.fori_loop(0, local_count, add_patch, (empty_grad, empty_light))]
    dynamic_slice x160 -> x0, local copies, waits for them, and re-layouts: 72.5 us -> none  [the longest x96 34.2 us: add_patch(): new_grad = old_grad + jnp.stack([patch_re[position], patch_im[position]])]
    psum x1, waiting for transfers between devices: 0.02 us -> 40 us  [shards(): grad_re, grad_im, obj_norm = lax.psum((grad_re, grad_im, obj_norm), 'scan')]
    dot_general x0 -> x3, matrix products: none -> 23.3 us  [the longest x1 14.9 us: shards(): jnp.einsum('pcjib,jkb->pcik', placed_rows, col_place, preferred_element_t...]
  transfers between devices with their start and end apart: 5 -> 4, of which waited for: 4 -> 4; matrix products, arithmetic and copies ran while one was open for 18% -> 4% of each run, Pallas kernels for 0% -> 0%
where the time goes in v1:
time: 751 us; the launch traced here: 740 us
  waiting for transfers between devices  493 us (66%)
  local copies, waits for them, and re-layouts  155 us (21%)
  matrix products  56.5 us (8%)
  other arithmetic  18.5 us (2%)
  between operations  15.2 us (2%)
    reduce_scatter x1, waiting for transfers between devices, shards(): lax.psum_scatter(grad_tile, 'mode', scatter_dimension=1, tiled=True)  218 us
    psum x1, waiting for transfers between devices, shards(): summed = lax.psum(jnp.concatenate([mode_intensity, own_light]), 'mode')  154 us
    gather x160, local copies, waits for them, and re-layouts  118 us
    all_gather x1, waiting for transfers between devices, shards(): every_mode = lax.all_gather(flat_mine, 'mode', axis=1, tiled=True)  81.5 us
    psum x1, waiting for transfers between devices, shards(): grad_re, grad_im, obj_norm = lax.psum((grad_re, grad_im, obj_norm), 'scan')  40 us
    slice x1, local copies, waits for them, and re-layouts, shards(): gathered_re = every_mode[0]  26.1 us
    dot_general x31, matrix products, highest_dot(): jnp.dot(left, right, precision=lax.Precision.HIGHEST, preferred_element_t...  18.8 us
  transfers between devices with their start and end apart: 4, of which 4 were waited for; matrix products, arithmetic and copies ran while one was open for 4% of the time, Pallas kernels for 0%

profile of v1, /device:TPU:2, one launch (start us, length us, event | category | flops | bytes accessed | tf_op | source)
XLA Modules:
  0.0 740.5 jit_solution(13497158749242758823)
XLA Ops:
  8.0 0.9 fusion.217
  9.1 118.6 %while.1 = (s32[]{:T(128)}, f32[2,256,1024]{2,1,0:T(8,128)}, s32[32,3]{0,1:T(4,128)S(1)}, f32[32,2,128,128]{2,3,0,1:T(8,128)}, s32[]{:T(128)}) while((s32[]{:T(128)}, f32[2,256,1024]{2,1,0:T(8,128)}, s32[32,3]{0,1:T(4,128)S(1)}, f32[32,2,128,128]{2,3,0,1:T(8,128)}, s32[]{:T(128)}) %tuple.46), condition=%wide.while_cond, body=%wide.while_body.sunk | while | flops 2 | bytes 786557 | solution.py:113
  9.7 2.3 dynamic-slice_bitcast_fusion.2
  13.4 2.3 dynamic-slice_bitcast_fusion.2
  17.1 2.3 dynamic-slice_bitcast_fusion.2
  20.8 2.3 dynamic-slice_bitcast_fusion.2
  24.5 2.3 dynamic-slice_bitcast_fusion.2
  28.2 2.3 dynamic-slice_bitcast_fusion.2
  31.9 2.3 dynamic-slice_bitcast_fusion.2
  35.6 2.3 dynamic-slice_bitcast_fusion.2
  39.4 2.3 dynamic-slice_bitcast_fusion.2
  43.1 2.3 dynamic-slice_bitcast_fusion.2
  46.7 2.3 dynamic-slice_bitcast_fusion.2
  50.4 2.3 dynamic-slice_bitcast_fusion.2
  54.2 2.3 dynamic-slice_bitcast_fusion.2
  57.9 2.3 dynamic-slice_bitcast_fusion.2
  61.6 2.3 dynamic-slice_bitcast_fusion.2
  65.3 2.3 dynamic-slice_bitcast_fusion.2
  69.0 2.3 dynamic-slice_bitcast_fusion.2
  72.7 2.3 dynamic-slice_bitcast_fusion.2
  76.4 2.3 dynamic-slice_bitcast_fusion.2
  80.1 2.3 dynamic-slice_bitcast_fusion.2
  83.8 2.3 dynamic-slice_bitcast_fusion.2
  87.5 2.3 dynamic-slice_bitcast_fusion.2
  91.2 2.3 dynamic-slice_bitcast_fusion.2
  94.9 2.3 dynamic-slice_bitcast_fusion.2
  98.7 2.3 dynamic-slice_bitcast_fusion.2
  102.4 2.3 dynamic-slice_bitcast_fusion.2
  106.0 2.3 dynamic-slice_bitcast_fusion.2
  109.8 2.3 dynamic-slice_bitcast_fusion.2
  113.5 2.3 dynamic-slice_bitcast_fusion.2
  117.2 2.3 dynamic-slice_bitcast_fusion.2
  120.9 2.3 dynamic-slice_bitcast_fusion.2
  124.6 2.3 dynamic-slice_bitcast_fusion.2
  127.7 2.8 fusion.44
  135.4 2.2 fusion.38
  137.6 1.5 pad_maximum_fusion.1
  139.3 2.9 copy.40
  142.4 154.0 %all-reduce.4.cloned.1.call-done = f32[33,128,128]{1,2,0:T(8,128)} async-done(((f32[33,128,128]{1,2,0:T(8,128)}), f32[33,128,128]{1,2,0:T(8,128)}) %all-reduce.4.cloned.1.call-update) | async-done | bytes 2162704 | tf_op jit(solution)/shard_map/psum | solution.py:124
  296.4 4.0 fusion.40
  305.3 1.5 copy-done.2
  306.7 2.7 fusion.35
  309.8 3.1 fusion.26
  313.2 5.2 fusion.320
  318.4 14.9 %bitcast_reduce_fusion = f32[2,256,1024]{2,1,0:T(8,128)} fusion(s32[32,128]{1,0:T(8,128)S(1)} %get-tuple-element.62, bf16[3,2,32,256,128]{4,3,2,1,0:T(8,128)(2,1)S(1)} %fusion.320), kind=kOutput, calls=%fused_computation.19 | convolution fusion | flops 12890144768 | bytes 14696448 | tf_op jit(solution)/shard_map/pcjib,jkb->pcik/dot_general | solution.py:147
  333.8 40.0 %all-reduce.6.cloned.1.call-done = (f32[128,128]{0,1:T(8,128)}, f32[128,128]{0,1:T(8,128)}, f32[128,128]{0,1:T(8,128)}) async-done(((f32[128,128]{0,1:T(8,128)}, f32[128,128]{0,1:T(8,128)}, f32[128,128]{0,1:T(8,128)}), (f32[128,128]{0,1:T(8,128)}, f32[128,128]{0,1:T(8,128)}, f32[128,128]{0,1:T(8,128)})) %all-reduce.6.cloned.1.call-update) | async-done | bytes 196624 | tf_op jit(solution)/shard_map/psum | solution.py:136
  373.8 0.9 divide_add_fusion.1
  375.0 0.8 pad_maximum_fusion.2
  375.8 0.9 subtract_convert_fusion.3
  376.7 3.2 fusion.61
  379.9 217.8 %reduce-scatter.2.cloned.1.call-done = f32[2,8,1024]{2,1,0:T(8,128)} async-done(((f32[2,256,1024]{2,1,0:T(8,128)}), f32[2,8,1024]{2,1,0:T(8,128)}) %reduce-scatter.2.cloned.1.call-update) | async-done | bytes 65552 | tf_op jit(solution)/shard_map/reduce_scatter | solution.py:158
  597.7 1.5 divide_add_fusion.2
  599.2 81.5 %all-gather.3.cloned.1.call-done = f32[2,524288]{1,0:T(2,128)} async-done(((f32[2,16384]{1,0:T(2,128)}), f32[2,524288]{1,0:T(2,128)}) %all-gather.3.cloned.1.call-update) | async-done | bytes 4194320 | tf_op jit(solution)/shard_map/all_gather | solution.py:162
  680.8 26.1 %slice_reduce_fusion.1 = (f32[524288]{0:T(1024)}, f32[524288]{0:T(1024)}) fusion(f32[2,524288]{1,0:T(2,128)} %all-gather.3.cloned.1.call-done), kind=kLoop, calls=%fused_computation.29 | loop fusion | bytes 8388608 | tf_op jit(solution)/shard_map/slice | solution.py:163
  706.9 1.7 squeeze.25
  708.6 1.8 fusion.222
  710.4 2.9 squeeze.26
  713.4 3.5 fusion.223
  716.9 1.8 convolution_add_fusion.2
  719.6 3.4 fusion.219
  728.6 1.1 fusion.145
  729.7 1.1 fusion.143
  730.9 1.1 fusion.139
  732.0 1.1 fusion.141
  (204 shorter events, 62.1 us)
Async XLA Ops:
  7.2 289.3 %all-reduce.4.cloned.1.call-start = ((), (), s32[]{:S(2)}) async-start(), calls=%async_computation.1 | async-start | bytes 4325376 | tf_op jit(solution)/shard_map/psum | solution.py:124
  139.1 234.7 %all-reduce.6.cloned.1.call-start = ((), (), s32[]{:S(2)}) async-start(), calls=%async_computation.4 | async-start | bytes 393216 | tf_op jit(solution)/shard_map/psum | solution.py:136
  139.3 2.9 copy-start.3
  304.5 2.2 copy-start.2
  313.0 284.7 %reduce-scatter.2.cloned.1.call-start = ((), (), s32[]{:S(2)}) async-start(), calls=%async_computation.2 | async-start | bytes 2162688 | tf_op jit(solution)/shard_map/reduce_scatter | solution.py:158
  333.4 347.4 %all-gather.3.cloned.1.call-start = ((), (), s32[]{:S(2)}) async-start(), calls=%async_computation.3 | async-start | bytes 4325376 | tf_op jit(solution)/shard_map/all_gather | solution.py:162
  713.3 3.6 copy-start
  725.2 4.6 copy-start.1
Sparse Core Ops, SparseCore 0:
  139.2 157.1 all-reduce.3
  313.1 60.6 all-reduce.5
  377.7 219.9 reduce-scatter.1
  600.7 79.9 all-gather.2

commit v2 on v1

--- a/solution.py
+++ b/solution.py
@@ -107,14 +107,18 @@
     row_starts = scan_offsets[0]
     col_starts = scan_offsets[1]
     local_count = row_starts.shape[0]
-    zero_index = jnp.zeros((), jnp.int32)
 
-    def cut_patch(row_start, col_start):
-        return lax.dynamic_slice(object_field, (zero_index, row_start, col_start), (2, M, M))
-
-    obj_patches = jax.vmap(cut_patch)(row_starts, col_starts)
-    obj_re = obj_patches[:, 0]
-    obj_im = obj_patches[:, 1]
+    col_place = onehot_place(col_starts, object_field.shape[2], M)
+    row_place = onehot_place(row_starts, object_field.shape[1], M)
+    field_parts = split_parts(object_field)
+    picked_cols = jnp.einsum(
+        "pcik,jkb->pcijb", field_parts, col_place, preferred_element_type=jnp.float32
+    ).astype(jnp.bfloat16)
+    obj_patches = jnp.einsum(
+        "jia,pcijb->pcjab", row_place, picked_cols, preferred_element_type=jnp.float32
+    ).sum(axis=0)
+    obj_re = obj_patches[0]
+    obj_im = obj_patches[1]
     obj_norm = jnp.sum(obj_re * obj_re + obj_im * obj_im, axis=0)
     wave_re = (probe_re * obj_re - probe_im * obj_im).astype(jnp.bfloat16)
     wave_im = (probe_re * obj_im + probe_im * obj_re).astype(jnp.bfloat16)
@@ -138,8 +142,6 @@
     step_im = probe_im + grad_im / (obj_norm + EPSILON)
 
     rows_share = object_field.shape[1] // lax.axis_size("mode")
-    col_place = onehot_place(col_starts, object_field.shape[2], M)
-    row_place = onehot_place(row_starts, object_field.shape[1], M)
     patch_parts = split_parts(jnp.stack([patch_re, patch_im]))
     placed_rows = jnp.einsum(
         "jia,pcjab->pcjib", row_place, patch_parts, preferred_element_type=jnp.float32
@@ -155,11 +157,13 @@
     light_rows = jnp.einsum(
         "pjib,jkb->pik", light_rows, col_place, preferred_element_type=jnp.float32
     ).sum(axis=0)[None]
-    grad_rows = lax.psum_scatter(grad_tile, "mode", scatter_dimension=1, tiled=True)
     own_rows = lax.dynamic_slice_in_dim(object_field, mode_index * rows_share, rows_share, 1)
-    object_new = own_rows + grad_rows / jnp.maximum(light_rows, FLOOR_ILLUM)
     flat_mine = jnp.stack([step_re.reshape(-1), step_im.reshape(-1)])[:, None, :]
     every_mode = lax.all_gather(flat_mine, "mode", axis=1, tiled=True)
+    mode_count = lax.axis_size("mode")
+    grad_blocks = grad_tile.reshape(2, mode_count, rows_share, grad_tile.shape[2])
+    grad_rows = lax.all_to_all(grad_blocks, "mode", 1, 1, tiled=False).sum(axis=1)
+    object_new = own_rows + grad_rows / jnp.maximum(light_rows, FLOOR_ILLUM)
     gathered_re = every_mode[0]
     gathered_im = every_mode[1]
     gram_re, gram_im = gram_of(gathered_re, gathered_im)

time: 751 us -> 452 us (0.60)
  the two profiles are of different devices: /device:TPU:2 before, /device:TPU:6 now
where the time goes in v2:
time: 452 us; the launch traced here: 445 us
  waiting for transfers between devices  283 us (63%)
  matrix products  74.6 us (17%)
  local copies, waits for them, and re-layouts  43.7 us (10%)
  other arithmetic  18.4 us (4%)
  between operations  15.3 us (3%)
  starting transfers between devices  10.3 us (2%)
    psum x1, waiting for transfers between devices, shards(): summed = lax.psum(jnp.concatenate([mode_intensity, own_light]), 'mode')  154 us
    psum x1, waiting for transfers between devices, shards(): grad_re, grad_im, obj_norm = lax.psum((grad_re, grad_im, obj_norm), 'scan')  60.8 us
    all_to_all x1, waiting for transfers between devices, shards(): lax.all_to_all(grad_blocks, 'mode', 1, 1, tiled=False).sum(axis=1)  55.8 us
    slice x1, local copies, waits for them, and re-layouts, shards(): gathered_re = every_mode[0]  26.1 us
    dot_general x1, matrix products, shards(): jnp.einsum('jia,pcijb->pcjab', row_place, picked_cols, preferred_element_...  19.1 us
    dot_general x31, matrix products, highest_dot(): jnp.dot(left, right, precision=lax.Precision.HIGHEST, preferred_element_t...  18.8 us
    dot_general x1, matrix products, shards(): jnp.einsum('pcjib,jkb->pcik', placed_rows, col_place, preferred_element_t...  13.6 us
    all_gather x1, waiting for transfers between devices, shards(): every_mode = lax.all_gather(flat_mine, 'mode', axis=1, tiled=True)  11.6 us
  transfers between devices with their start and end apart: 4, of which 4 were waited for; matrix products, arithmetic and copies ran while one was open for 7% of the time, Pallas kernels for 0%

profile of v2, /device:TPU:6, one launch (start us, length us, event | category | flops | bytes accessed | tf_op | source)
XLA Modules:
  0.0 444.7 jit_solution(101525939191666022)
XLA Ops:
  7.2 0.8 slice_bitcast_fusion.2
  8.0 0.9 fusion.243
  9.1 3.0 convert_bitcast_fusion
  12.1 19.1 %fusion.36 = f32[32,2,128,128]{3,2,1,0:T(8,128)} fusion(s32[32,128]{1,0:T(8,128)S(1)} %get-tuple-element.45, bf16[1,2,256,1024]{3,2,1,0:T(8,128)(2,1)S(1)} %get-tuple-element.26, bf16[1,2,256,1024]{3,2,1,0:T(8,128)(2,1)S(1)} %get-tuple-element.27, bf16[1,2,256,1024]{3,2,1,0:T(8,128)(2,1)S(1)} %get-tuple-element.25, s32[32,128]{1,0:T(8,128)S(1)} %get-tuple-element.44), kind=kOutput, calls=%fused_computation.30 | convolution fusion | flops 14518583296 | bytes 7372800 | tf_op jit(solution)/shard_map/jia,pcijb->pcjab/dot_general | solution.py:117
  31.2 2.5 copy.132
  33.7 0.6 add_convert_fusion.2
  34.3 1.3 copy-done.2
  35.6 0.7 fusion.128
  36.3 0.7 fusion.143
  37.0 0.7 subtract_convert_fusion.2
  37.7 0.7 fusion.125
  38.4 0.7 fusion.141
  39.1 0.7 add_convert_fusion.1
  39.7 0.7 convolution_subtract_fusion.1
  40.4 2.2 fusion.65
  42.6 1.5 pad_maximum_fusion.1
  44.2 3.1 copy.86
  47.3 154.2 %all-reduce.4.cloned.1.call-done = f32[33,128,128]{1,2,0:T(8,128)} async-done(((f32[33,128,128]{1,2,0:T(8,128)}), f32[33,128,128]{1,2,0:T(8,128)}) %all-reduce.4.cloned.1.call-update) | async-done | bytes 2162704 | tf_op jit(solution)/shard_map/psum | solution.py:128
  201.6 4.0 fusion.67
  205.6 0.7 fusion.137
  206.2 0.7 fusion.133
  206.9 0.7 add_convert_fusion
  207.6 0.7 subtract_convert_fusion.1
  208.3 0.7 fusion.131
  209.0 0.7 fusion.135
  209.7 0.7 convolution_subtract_fusion
  210.4 1.5 copy-done.3
  211.9 4.1 fusion.62
  216.0 60.8 %all-reduce.6.cloned.1.call-done = (f32[128,128]{0,1:T(8,128)}, f32[128,128]{0,1:T(8,128)}, f32[128,128]{0,1:T(8,128)}) async-done(((f32[128,128]{0,1:T(8,128)}, f32[128,128]{0,1:T(8,128)}, f32[128,128]{0,1:T(8,128)}), (f32[128,128]{0,1:T(8,128)}, f32[128,128]{0,1:T(8,128)}, f32[128,128]{0,1:T(8,128)})) %all-reduce.6.cloned.1.call-update) | async-done | bytes 196624 | tf_op jit(solution)/shard_map/psum | solution.py:140
  276.9 0.9 divide_add_fusion.1
  278.0 0.8 pad_maximum_fusion.2
  278.8 2.1 fusion.35
  281.0 1.2 fusion.53
  282.2 4.1 fusion.346
  286.3 13.6 %bitcast_reduce_fusion = f32[2,256,1024]{2,1,0:T(8,128)S(1)} fusion(s32[32,128]{1,0:T(8,128)S(1)} %get-tuple-element.45, bf16[3,2,32,256,128]{3,4,2,1,0:T(8,128)(2,1)S(1)} %fusion.346), kind=kOutput, calls=%fused_computation.21 | convolution fusion | flops 12890144768 | bytes 14696448 | tf_op jit(solution)/shard_map/pcjib,jkb->pcik/dot_general | solution.py:149
  299.8 1.6 copy.96
  301.4 10.2 %all-to-all-start = ((f32[2,32,8,1024]{3,2,0,1:T(8,128)}), f32[2,32,8,1024]{3,2,0,1:T(8,128)S(1)}, u32[]{:S(2)}, u32[]{:S(2)}) async-start(f32[2,32,8,1024]{3,2,0,1:T(8,128)} %copy.96), calls=%async_computation | async-start | bytes 4194304 | tf_op jit(solution)/shard_map/all_to_all | solution.py:165
  311.7 0.9 subtract_convert_fusion.5
  312.6 3.2 fusion.85
  315.9 55.8 %all-to-all-done = f32[2,32,8,1024]{3,2,0,1:T(8,128)S(1)} async-done(((f32[2,32,8,1024]{3,2,0,1:T(8,128)}), f32[2,32,8,1024]{3,2,0,1:T(8,128)S(1)}, u32[]{:S(2)}, u32[]{:S(2)}) %all-to-all-start) | async-done | bytes 2097184 | tf_op jit(solution)/shard_map/all_to_all | solution.py:165
  371.8 1.5 divide_add_fusion.2
  373.3 11.6 %all-gather.3.cloned.1.call-done = f32[2,524288]{1,0:T(2,128)} async-done(((f32[2,16384]{1,0:T(2,128)}), f32[2,524288]{1,0:T(2,128)}) %all-gather.3.cloned.1.call-update) | async-done | bytes 4194320 | tf_op jit(solution)/shard_map/all_gather | solution.py:162
  384.9 26.1 %slice_reduce_fusion.1 = (f32[524288]{0:T(1024)}, f32[524288]{0:T(1024)}) fusion(f32[2,524288]{1,0:T(2,128)} %all-gather.3.cloned.1.call-done), kind=kLoop, calls=%fused_computation.39 | loop fusion | bytes 8388608 | tf_op jit(solution)/shard_map/slice | solution.py:167
  411.0 1.7 squeeze.18
  412.8 1.8 fusion.248
  414.5 3.0 squeeze.19
  417.5 3.5 fusion.249
  421.1 1.8 convolution_add_fusion.2
  422.9 0.7 gather_fusion
  423.7 3.4 fusion.245
  427.1 0.7 multiply_reduce_fusion
  428.6 0.2 fusion.95
  428.8 0.2 fusion.147
  429.2 0.2 fusion.94
  429.7 0.2 fusion.93
  430.2 0.2 fusion.92
  431.2 0.2 fusion.90
  432.2 0.2 fusion.88
  432.6 0.2 fusion.145
  432.8 1.1 fusion.170
  433.9 1.1 fusion.168
  435.0 1.1 fusion.164
  436.1 1.1 fusion.166
  437.3 0.7 pad_maximum_fusion.3
  (48 shorter events, 3.6 us)
Async XLA Ops:
  7.2 194.4 %all-reduce.4.cloned.1.call-start = ((), (), s32[]{:S(2)}) async-start(), calls=%async_computation.1 | async-start | bytes 4325376 | tf_op jit(solution)/shard_map/psum | solution.py:128
  33.7 1.9 copy-start.2
  44.2 232.7 %all-reduce.6.cloned.1.call-start = ((), (), s32[]{:S(2)}) async-start(), calls=%async_computation.3 | async-start | bytes 393216 | tf_op jit(solution)/shard_map/psum | solution.py:140
  209.7 2.2 copy-start.3
  216.0 168.9 %all-gather.3.cloned.1.call-start = ((), (), s32[]{:S(2)}) async-start(), calls=%async_computation.2 | async-start | bytes 4325376 | tf_op jit(solution)/shard_map/all_gather | solution.py:162
  278.8 2.2 copy-start.4
  301.4 10.2 %copy-start.5 = (s32[2,32]{1,0:T(2,128)S(1)}, s32[2,32]{1,0:T(2,128)}, u32[]{:S(2)}) copy-start(s32[2,32]{1,0:T(2,128)} %param.6) | copy-start | bytes 772
  301.4 70.2 %all-to-all-start = ((f32[2,32,8,1024]{3,2,0,1:T(8,128)}), f32[2,32,8,1024]{3,2,0,1:T(8,128)S(1)}, u32[]{:S(2)}, u32[]{:S(2)}) async-start(f32[2,32,8,1024]{3,2,0,1:T(8,128)} %copy.96), calls=%async_computation | async-start | bytes 4194304 | tf_op jit(solution)/shard_map/all_to_all | solution.py:165
  417.5 3.6 copy-start
  429.3 4.6 %copy-start.1 = (f32[32,16384]{1,0:T(8,128)S(1)}, f32[32,16384]{1,0:T(8,128)}, u32[]{:S(2)}) copy-start(f32[32,16384]{1,0:T(8,128)} %squeeze.19) | copy-start | bytes 6291460
Sparse Core Ops, SparseCore 0:
  44.3 157.2 all-reduce.3
  216.1 60.7 all-reduce.5
  280.0 104.8 all-gather.2

commit v3 on v2

--- a/solution.py
+++ b/solution.py
@@ -97,6 +97,14 @@
     middle = rest.astype(jnp.bfloat16)
     low = (rest - middle.astype(jnp.float32)).astype(jnp.bfloat16)
     return jnp.stack([high, middle, low])
+
+
+def exchange_sum(values, axis_name):
+    count = lax.axis_size(axis_name)
+    pieces = values.reshape(count, -1)
+    mine = lax.all_to_all(pieces, axis_name, 0, 0, tiled=False).sum(axis=0)
+    spread = jnp.broadcast_to(mine[None], pieces.shape)
+    return lax.all_to_all(spread, axis_name, 0, 0, tiled=False).reshape(values.shape)
 
 
 def shards(object_field, probe_modes, scan_offsets, measured):
@@ -125,7 +133,7 @@
     far_re, far_im = forward_pass(wave_re, wave_im, cos_t, sin_t)
     mode_intensity = far_re * far_re + far_im * far_im
     own_light = (probe_re * probe_re + probe_im * probe_im)[None]
-    summed = lax.psum(jnp.concatenate([mode_intensity, own_light]), "mode")
+    summed = exchange_sum(jnp.concatenate([mode_intensity, own_light]), "mode")
     intensity = summed[:local_count]
     light_patch = summed[local_count:]
     amp_ratio = jnp.sqrt(measured / jnp.maximum(intensity, FLOOR_INTENSITY))
@@ -137,9 +145,6 @@
     grad_im = jnp.sum(obj_re * back_im - obj_im * back_re, axis=0)
     patch_re = probe_re * back_re + probe_im * back_im
     patch_im = probe_re * back_im - probe_im * back_re
-    grad_re, grad_im, obj_norm = lax.psum((grad_re, grad_im, obj_norm), "scan")
-    step_re = probe_re + grad_re / (obj_norm + EPSILON)
-    step_im = probe_im + grad_im / (obj_norm + EPSILON)
 
     rows_share = object_field.shape[1] // lax.axis_size("mode")
     patch_parts = split_parts(jnp.stack([patch_re, patch_im]))
@@ -158,6 +163,11 @@
         "pjib,jkb->pik", light_rows, col_place, preferred_element_type=jnp.float32
     ).sum(axis=0)[None]
     own_rows = lax.dynamic_slice_in_dim(object_field, mode_index * rows_share, rows_share, 1)
+    grad_sums = jnp.stack([grad_re, grad_im, obj_norm])
+    grad_sums, grad_tile = lax.optimization_barrier((grad_sums, grad_tile))
+    grad_sums = exchange_sum(grad_sums, "scan")
+    step_re = probe_re + grad_sums[0] / (grad_sums[2] + EPSILON)
+    step_im = probe_im + grad_sums[1] / (grad_sums[2] + EPSILON)
     flat_mine = jnp.stack([step_re.reshape(-1), step_im.reshape(-1)])[:, None, :]
     every_mode = lax.all_gather(flat_mine, "mode", axis=1, tiled=True)
     mode_count = lax.axis_size("mode")

time: 452 us -> 392 us (0.87)
  the two profiles are of different devices: /device:TPU:6 before, /device:TPU:2 now
where the time goes in v3:
time: 392 us; the launch traced here: 384 us
  waiting for transfers between devices  120 us (31%)
  blocking collectives  84.9 us (22%)
  matrix products  78 us (20%)
  local copies, waits for them, and re-layouts  55.2 us (14%)
  other arithmetic  18.9 us (5%)
  between operations  15.7 us (4%)
  starting transfers between devices  10.9 us (3%)
    all_to_all x2, blocking collectives, exchange_sum(): mine = lax.all_to_all(pieces, axis_name, 0, 0, tiled=False).sum(axis=0)  75.7 us
    all_to_all x1, waiting for transfers between devices, shards(): lax.all_to_all(grad_blocks, 'mode', 1, 1, tiled=False).sum(axis=1)  54 us
    all_to_all x1, waiting for transfers between devices, exchange_sum(): lax.all_to_all(spread, axis_name, 0, 0, tiled=False).reshape(values.shape)  47.1 us
    slice x1, local copies, waits for them, and re-layouts, shards(): gathered_re = every_mode[0]  26.1 us
    all_gather x1, waiting for transfers between devices, shards(): every_mode = lax.all_gather(flat_mine, 'mode', axis=1, tiled=True)  19.4 us
    dot_general x1, matrix products, shards(): jnp.einsum('jia,pcijb->pcjab', row_place, picked_cols, preferred_element_...  19.1 us
    dot_general x31, matrix products, highest_dot(): jnp.dot(left, right, precision=lax.Precision.HIGHEST, preferred_element_t...  18.8 us
    dot_general x1, matrix products, shards(): jnp.einsum('pcjib,jkb->pcik', placed_rows, col_place, preferred_element_t...  16.7 us
  transfers between devices with their start and end apart: 3, of which 3 were waited for; matrix products, arithmetic and copies ran while one was open for 3% of the time, Pallas kernels for 0%

profile of v3, /device:TPU:2, one launch (start us, length us, event | category | flops | bytes accessed | tf_op | source)
XLA Modules:
  0.0 384.1 jit_solution(16535463285167358465)
XLA Ops:
  7.2 0.8 slice_bitcast_fusion.2
  7.9 0.9 fusion.240
  9.0 2.9 convert_bitcast_fusion
  12.0 19.1 %fusion.36 = f32[32,2,128,128]{3,2,1,0:T(8,128)} fusion(s32[32,128]{1,0:T(8,128)S(1)} %get-tuple-element.47, bf16[1,2,256,1024]{3,2,1,0:T(8,128)(2,1)S(1)} %get-tuple-element.28, bf16[1,2,256,1024]{3,2,1,0:T(8,128)(2,1)S(1)} %get-tuple-element.29, bf16[1,2,256,1024]{3,2,1,0:T(8,128)(2,1)S(1)} %get-tuple-element.27, s32[32,128]{1,0:T(8,128)S(1)} %get-tuple-element.46), kind=kOutput, calls=%fused_computation.30 | convolution fusion | flops 14518583296 | bytes 7372800 | tf_op jit(solution)/shard_map/jia,pcijb->pcjab/dot_general | solution.py:125
  31.1 2.5 copy.139
  33.6 0.6 add_convert_fusion.2
  34.2 1.3 copy-done.2
  35.5 0.7 fusion.125
  36.2 0.7 fusion.140
  36.9 0.7 subtract_convert_fusion.2
  37.6 0.7 fusion.122
  38.3 0.7 fusion.138
  39.0 0.7 add_convert_fusion.1
  39.7 0.7 convolution_subtract_fusion.1
  40.4 2.2 fusion.62
  42.5 1.5 pad_maximum_fusion.1
  44.1 3.0 copy.90
  47.0 65.8 %all_to_all.35 = f32[32,1,16896]{2,1,0:T(1,128)} all-to-all(f32[32,1,16896]{2,1,0:T(1,128)} %bitcast.311), channel_id=1, replica_groups=mesh['scan'=8,'mode'=32] {'mode'}, dimensions={0} | all-to-all | bytes 4325376 | tf_op jit(solution)/shard_map/all_to_all | solution.py:105
  112.8 2.8 reduce_sum.94
  115.7 2.4 broadcast_in_dim.8
  118.1 4.8 %all-to-all-start.1 = ((f32[32,1,16896]{2,1,0:T(1,128)}), f32[32,1,16896]{2,1,0:T(1,128)}, u32[]{:S(2)}, u32[]{:S(2)}) async-start(f32[32,1,16896]{2,1,0:T(1,128)} %broadcast_in_dim.8), calls=%async_computation.1 | async-start | bytes 4325376 | tf_op jit(solution)/shard_map/all_to_all | solution.py:107
  123.0 3.4 copy.93
  126.3 47.1 %all-to-all-done.1 = f32[32,1,16896]{2,1,0:T(1,128)} async-done(((f32[32,1,16896]{2,1,0:T(1,128)}), f32[32,1,16896]{2,1,0:T(1,128)}, u32[]{:S(2)}, u32[]{:S(2)}) %all-to-all-start.1) | async-done | bytes 2162720 | tf_op jit(solution)/shard_map/all_to_all | solution.py:107
  173.4 3.1 slice.67
  176.5 2.9 copy.137
  179.5 4.0 %fusion.64 = (bf16[32,128,128]{1,2,0:T(8,128)(2,1)S(1)}, bf16[32,128,128]{1,2,0:T(8,128)(2,1)S(1)}) fusion(f32[32,128,128]{2,1,0:T(8,128)S(1)} %convolution_subtract_fusion.1, f32[32,128,128]{1,2,0:T(8,128)} %copy.93, f32[32,128,128]{1,2,0:T(8,128)} %copy.137, f32[32,128,128]{2,1,0:T(8,128)} %get-tuple-element.43), kind=kLoop, calls=%fused_computation.64 | loop fusion | flops 3670016 | bytes 10485760 | tf_op jit(solution)/shard_map/convert_element_type | solution.py:141
  183.4 0.7 fusion.134
  184.1 0.7 fusion.130
  184.8 0.7 add_convert_fusion
  185.5 0.7 subtract_convert_fusion.1
  186.2 0.7 fusion.128
  186.9 0.7 fusion.132
  187.6 0.7 convolution_subtract_fusion
  188.3 1.5 copy-done.3
  189.8 2.1 fusion.59
  191.9 0.4 fusion.35
  192.2 1.2 fusion.53
  193.4 6.4 %fusion.343 = bf16[3,2,32,256,128]{3,4,2,1,0:T(8,128)(2,1)} fusion(bf16[1,2,32,128,128]{3,4,2,1,0:T(8,128)(2,1)S(1)} %get-tuple-element.21, bf16[1,2,32,128,128]{3,4,2,1,0:T(8,128)(2,1)S(1)} %get-tuple-element.20, bf16[1,2,32,128,128]{3,4,2,1,0:T(8,128)(2,1)S(1)} %fusion.35, s32[32,128]{1,0:T(8,128)S(1)} %get-tuple-element.46), kind=kOutput, calls=%fused_computation.8.clone.clone.clone.2 | convolution fusion | flops 1624244224 | bytes 18890752 | tf_op jit(solution)/shard_map/jia,pcjab->pcjib/dot_general | solution.py:151
  199.8 16.7 %bitcast_reduce_fusion = f32[2,256,1024]{2,1,0:T(8,128)S(1)} fusion(s32[32,128]{1,0:T(8,128)S(1)} %get-tuple-element.47, bf16[3,2,32,256,128]{3,4,2,1,0:T(8,128)(2,1)} %fusion.343), kind=kOutput, calls=%fused_computation.21 | convolution fusion | flops 12890144768 | bytes 14696448 | tf_op jit(solution)/shard_map/pcjib,jkb->pcik/dot_general | solution.py:154
  216.6 10.0 %all_to_all.36 = f32[8,1,6144]{2,1,0:T(1,128)S(1)} all-to-all(f32[8,1,6144]{2,1,0:T(1,128)S(1)} %bitcast.318), channel_id=1, replica_groups=mesh['scan'=8,'mode'=32] {'scan'}, dimensions={0} | all-to-all | bytes 393216 | tf_op jit(solution)/shard_map/all_to_all | solution.py:105
  226.8 9.2 %all_to_all.37 = f32[8,1,6144]{2,1,0:T(1,128)S(1)} all-to-all(f32[8,1,6144]{2,1,0:T(1,128)S(1)} %broadcast_in_dim.9), channel_id=1, replica_groups=mesh['scan'=8,'mode'=32] {'scan'}, dimensions={0} | all-to-all | bytes 393216 | tf_op jit(solution)/shard_map/all_to_all | solution.py:107
  236.2 0.8 pad_maximum_fusion.3
  237.0 1.5 copy.103
  238.5 6.1 %all-to-all-start.2 = ((f32[2,32,8,1024]{3,2,0,1:T(8,128)}), f32[2,32,8,1024]{3,2,0,1:T(8,128)S(1)}, u32[]{:S(2)}, u32[]{:S(2)}) async-start(f32[2,32,8,1024]{3,2,0,1:T(8,128)} %copy.103), calls=%async_computation.2 | async-start | bytes 4194304 | tf_op jit(solution)/shard_map/all_to_all | solution.py:175
  244.7 0.9 subtract_convert_fusion.5
  245.6 3.2 fusion.82
  248.8 54.0 %all-to-all-done.2 = f32[2,32,8,1024]{3,2,0,1:T(8,128)S(1)} async-done(((f32[2,32,8,1024]{3,2,0,1:T(8,128)}), f32[2,32,8,1024]{3,2,0,1:T(8,128)S(1)}, u32[]{:S(2)}, u32[]{:S(2)}) %all-to-all-start.2) | async-done | bytes 2097184 | tf_op jit(solution)/shard_map/all_to_all | solution.py:175
  303.0 1.5 divide_add_fusion
  304.5 19.4 %all-gather.3.cloned.1.call-done = f32[2,524288]{1,0:T(2,128)} async-done(((f32[2,16384]{1,0:T(2,128)}), f32[2,524288]{1,0:T(2,128)}) %all-gather.3.cloned.1.call-update) | async-done | bytes 4194320 | tf_op jit(solution)/shard_map/all_gather | solution.py:172
  323.8 26.1 %slice_reduce_fusion.1 = (f32[524288]{0:T(1024)}, f32[524288]{0:T(1024)}) fusion(f32[2,524288]{1,0:T(2,128)} %all-gather.3.cloned.1.call-done), kind=kLoop, calls=%fused_computation.39 | loop fusion | bytes 8388608 | tf_op jit(solution)/shard_map/slice | solution.py:177
  350.0 1.7 squeeze.28
  351.7 1.8 fusion.245
  353.5 3.0 squeeze.29
  356.5 3.5 fusion.246
  360.0 1.8 convolution_add_fusion.2
  361.9 0.7 gather_fusion
  362.7 3.4 fusion.242
  366.1 0.7 multiply_reduce_fusion
  367.8 0.2 fusion.144
  371.8 1.1 fusion.167
  372.9 1.1 fusion.165
  374.0 1.1 fusion.161
  375.1 1.1 fusion.163
  376.2 0.7 pad_maximum_fusion.4
  (54 shorter events, 5.0 us)
Async XLA Ops:
  33.6 1.9 copy-start.2
  118.1 55.3 %all-to-all-start.1 = ((f32[32,1,16896]{2,1,0:T(1,128)}), f32[32,1,16896]{2,1,0:T(1,128)}, u32[]{:S(2)}, u32[]{:S(2)}) async-start(f32[32,1,16896]{2,1,0:T(1,128)} %broadcast_in_dim.8), calls=%async_computation.1 | async-start | bytes 4325376 | tf_op jit(solution)/shard_map/all_to_all | solution.py:107
  122.9 200.9 %all-gather.3.cloned.1.call-start = ((), (), s32[]{:S(2)}) async-start(), calls=%async_computation.5 | async-start | bytes 4325376 | tf_op jit(solution)/shard_map/all_gather | solution.py:172
  187.6 2.2 copy-start.3
  238.5 6.1 %copy-start.4 = (s32[2,32]{1,0:T(2,128)S(1)}, s32[2,32]{1,0:T(2,128)}, u32[]{:S(2)}) copy-start(s32[2,32]{1,0:T(2,128)} %param.6) | copy-start | bytes 772
  238.5 64.4 %all-to-all-start.2 = ((f32[2,32,8,1024]{3,2,0,1:T(8,128)}), f32[2,32,8,1024]{3,2,0,1:T(8,128)S(1)}, u32[]{:S(2)}, u32[]{:S(2)}) async-start(f32[2,32,8,1024]{3,2,0,1:T(8,128)} %copy.103), calls=%async_computation.2 | async-start | bytes 4194304 | tf_op jit(solution)/shard_map/all_to_all | solution.py:175
  356.5 3.6 copy-start
  368.3 4.6 %copy-start.1 = (f32[32,16384]{1,0:T(8,128)S(1)}, f32[32,16384]{1,0:T(8,128)}, u32[]{:S(2)}) copy-start(f32[32,16384]{1,0:T(8,128)} %squeeze.29) | copy-start | bytes 6291460
Sparse Core Ops, SparseCore 0:
  237.1 86.6 all-gather.2
